TPU v7x, 256 devices: a whole 4x4x8 slice. The times are simulated.
256 devices in a mesh: expert: 16 (over z, core), tensor: 16 (over y, x).
Axes of the slice: x: 4, y: 4, z: 8, core: 2. Of those that a mesh axis runs over, the one named last changes fastest.
Arguments:
- residual_in: bfloat16 [22528, 1024], P(('expert', 'tensor')), may hold values from -6 to 6
- attn_heads: bfloat16 [1024, 22528], P('tensor', 'expert'), may hold values from -6 to 6
- out_proj: bfloat16 [1024, 1024], P('tensor'), may hold values from -0.1875 to 0.1875
- gain_first: float32 [1024], replicated, may hold values from 0.25 to 1.75
- router_weight: float32 [1024, 16], replicated, may hold values from -0.046875 to 0.046875
- routes: int32 [22528, 2], P(('expert', 'tensor')), may hold values from 0 to 15, all different within a row; in each aligned block of 88 rows (0 to 87, 88 to 175, ...) at most 22 rows name the same one
- w_gate: bfloat16 [16, 2816, 1024], P('expert', 'tensor'), may hold values from -0.1875 to 0.1875
- w_upward: bfloat16 [16, 2816, 1024], P('expert', 'tensor'), may hold values from -0.1875 to 0.1875
- w_downward: bfloat16 [16, 2816, 1024], P('expert', 'tensor'), may hold values from -0.21875 to 0.21875
- gain_second: float32 [1024], replicated, may hold values from 0.25 to 1.75
Outputs:
- residual_out: bfloat16 [22528, 1024], P(('expert', 'tensor'))
- next_normed: bfloat16 [22528, 1024], P(('expert', 'tensor'))
Inputs may be any that keep to these rules, and one draw needn't show every extreme that they name: `routes`: each row names two different experts; among the rows of one device no expert is named more than 22 times, and some expert reaches 22.
All inputs are finite; a program needn't handle non-finite values.
Results may differ from a plain program's by a relative error of at most 0.012.
Values may be sent and summed in bfloat16 or wider, within the bound.
No kernel may reach another device: no remote copies, remote signals or barrier semaphores. Data moves between devices by JAX's collectives and lax.ppermute only.
A program may use at most 128 MiB of HBM per device.

v0:
```python
import jax
import jax.numpy as jnp
from jax import lax
from jax.sharding import PartitionSpec as P


def rms_scale(values, gain):
    wide = values.astype(jnp.float32)
    scale = lax.rsqrt(jnp.mean(wide * wide, axis=-1, keepdims=True) + 1e-06)
    return (wide * scale * gain).astype(jnp.bfloat16)


def expert_block(inputs, gate_rows, up_rows, down_rows):
    gate_part = lax.dot_general(
        inputs, gate_rows, (((1,), (1,)), ((), ())), preferred_element_type=jnp.float32
    )
    up_part = lax.dot_general(
        inputs, up_rows, (((1,), (1,)), ((), ())), preferred_element_type=jnp.float32
    )
    hid = (jax.nn.gelu(gate_part, approximate=True) * up_part).astype(jnp.bfloat16)
    return jnp.dot(hid, down_rows, preferred_element_type=jnp.float32)


def per_device(
    residual_in,
    attn_heads,
    out_proj,
    gain_first,
    router_weight,
    routes,
    w_gate,
    w_upward,
    w_downward,
    gain_second,
):
    row_count = residual_in.shape[0]
    width = residual_in.shape[1]
    n_expert = lax.axis_size("expert")
    capacity = 4 * row_count // n_expert
    block = attn_heads
    projected = lax.psum_scatter(
        lax.dot_general(
            block, out_proj, (((0,), (0,)), ((), ())), preferred_element_type=jnp.float32
        ),
        "tensor",
        scatter_dimension=0,
        tiled=True,
    )
    hidden_one = (residual_in.astype(jnp.float32) + projected).astype(jnp.bfloat16)
    normed = rms_scale(hidden_one, gain_first)
    logits = jnp.dot(normed.astype(jnp.float32), router_weight, precision=lax.Precision.HIGHEST)
    router_probs = jax.nn.softmax(logits, axis=-1)
    picked = jnp.take_along_axis(router_probs, routes, axis=1)
    gate_weights = picked / jnp.sum(picked, axis=1, keepdims=True)
    flat_ids = routes.reshape(-1)
    expert_iota = jnp.arange(n_expert, dtype=jnp.int32)
    onehot = (flat_ids[:, None] == expert_iota[None, :]).astype(jnp.int32)
    earlier = jnp.cumsum(onehot, axis=0) - onehot
    slot_index = jnp.sum(earlier * onehot, axis=1)
    target = flat_ids * capacity + slot_index
    slot_iota = jnp.arange(n_expert * capacity, dtype=jnp.int32)
    placing = (slot_iota[:, None] == target[None, :]).astype(jnp.bfloat16)
    repeated = jnp.repeat(normed, 2, axis=0)
    send_slots = jnp.dot(placing, repeated, preferred_element_type=jnp.float32).astype(jnp.bfloat16)
    send_slots = send_slots.reshape(n_expert, capacity, width)
    received = lax.all_to_all(send_slots, "expert", split_axis=0, concat_axis=0, tiled=True)
    slot_total = n_expert * capacity
    rows_in = received.reshape(slot_total, width)
    gate_rows = w_gate[0]
    up_rows = w_upward[0]
    down_rows = w_downward[0]
    all_rows = lax.all_gather(rows_in, "tensor", axis=0, tiled=True)
    block = all_rows
    expert_sum = lax.psum_scatter(
        expert_block(block, gate_rows, up_rows, down_rows).astype(jnp.bfloat16),
        "tensor",
        scatter_dimension=0,
        tiled=True,
    )
    expert_out = expert_sum.reshape(n_expert, capacity, width)
    returned = lax.all_to_all(expert_out, "expert", split_axis=0, concat_axis=0, tiled=True)
    returned = returned.reshape(slot_total, width)
    per_route = lax.dot_general(
        placing, returned, (((0,), (0,)), ((), ())), preferred_element_type=jnp.float32
    )
    per_route = per_route.reshape(row_count, 2, width)
    mixed = jnp.sum(gate_weights[:, :, None] * per_route, axis=1)
    residual_out = (hidden_one.astype(jnp.float32) + mixed).astype(jnp.bfloat16)
    next_normed = rms_scale(residual_out, gain_second)
    return (residual_out, next_normed)


def solution(mesh):
    placed = (
        P(("expert", "tensor"), None),
        P("tensor", "expert"),
        P("tensor", None),
        P(),
        P(),
        P(("expert", "tensor"), None),
        P("expert", "tensor", None),
        P("expert", "tensor", None),
        P("expert", "tensor", None),
        P(),
    )
    return jax.shard_map(
        per_device,
        mesh=mesh,
        in_specs=placed,
        out_specs=(P(("expert", "tensor"), None), P(("expert", "tensor"), None)),
        check_vma=False,
    )
```

profile of v0, /device:TPU:1, one launch (start us, length us, event | category | flops | bytes accessed | tf_op | source)
XLA Modules:
  0.0 380.7 jit_solution(14872669456772548435)
XLA Ops:
  7.2 0.0 copy-start
  7.2 0.0 reduce-scatter.7.cloned.1.call-start
  7.2 4.4 %fusion.38 = f32[1408,1024]{1,0:T(8,128)} fusion(bf16[64,1408]{1,0:T(8,128)(2,1)} %param.11, bf16[64,1024]{1,0:T(8,128)(2,1)} %param.12), kind=kOutput, calls=%fused_computation.66 | convolution fusion | flops 184549376 | bytes 6078464 | tf_op jit(solution)/shard_map/dot_general | solution.py:42
  11.7 0.0 copy-start.5
  11.7 0.0 copy-start.3
  11.7 0.0 copy-start.6
  11.7 0.0 reduce-scatter.7.cloned.1.call-update
  11.7 0.0 all-gather.2.cloned.1.call-start
  11.7 0.6 copy-done.5
  12.3 0.1 copy.34
  12.4 0.1 reshape.109
  12.6 0.6 reduce-window.6
  13.2 0.2 slice_reduce_fusion
  13.4 0.1 bitcast_bitcast_fusion
  13.5 86.2 %reduce-scatter.7.cloned.1.call-done = f32[88,1024]{1,0:T(8,128)} async-done(((f32[1408,1024]{1,0:T(8,128)}), f32[88,1024]{1,0:T(8,128)}) %reduce-scatter.7.cloned.1.call-update) | async-done | bytes 360464
  99.7 0.0 copy-done.3
  99.7 1.1 fusion.16
  100.9 0.0 copy-done.6
  100.9 0.0 copy-start.2
  100.9 0.1 fusion.18
  101.0 0.2 broadcast_in_dim.7
  101.2 0.1 reshape.112
  101.4 0.3 convolution_convert_fusion.1
  101.7 0.2 reshape.113
  101.9 32.1 %all_to_all.10 = bf16[16,22,1024]{2,1,0:T(8,128)(2,1)S(1)} all-to-all(bf16[16,22,1024]{2,1,0:T(8,128)(2,1)S(1)} %reshape.113), channel_id=1, replica_groups=mesh['expert'=16,'tensor'=16] {'expert'}, dimensions={0} | all-to-all | bytes 1441792 | tf_op jit(solution)/shard_map/all_to_all | solution.py:66
  134.1 1.1 reshape.114
  135.1 0.0 all-gather.2.cloned.1.call-update
  135.1 0.0 copy-start.8
  135.2 0.0 reduce-scatter.5.cloned.1.call-start
  135.2 84.5 %all-gather.2.cloned.1.call-done = bf16[5632,1024]{1,0:T(8,128)(2,1)} async-done(((bf16[352,1024]{1,0:T(8,128)(2,1)}), bf16[5632,1024]{1,0:T(8,128)(2,1)}) %all-gather.2.cloned.1.call-update) | async-done | bytes 11534352 | tf_op jit(solution)/shard_map/all_gather | solution.py:72
  219.7 0.0 copy-done.2
  219.7 10.2 %fusion.23 = f32[5632,176]{0,1:T(8,128)} fusion(bf16[5632,1024]{1,0:T(8,128)(2,1)} %all-gather.2.cloned.1.call-done, bf16[1,176,1024]{2,1,0:T(8,128)(2,1)S(1)} %copy-done.2), kind=kOutput, calls=%fused_computation.33 | convolution fusion | flops 2030043136 | bytes 15859712 | tf_op jit(solution)/shard_map/dot_general | solution.py:14
  229.9 0.0 copy-done
  229.9 0.0 copy-done.8
  229.9 13.1 %convolution_convert_fusion = bf16[5632,1024]{1,0:T(8,128)(2,1)} fusion(bf16[5632,1024]{1,0:T(8,128)(2,1)} %all-gather.2.cloned.1.call-done, f32[5632,176]{0,1:T(8,128)} %fusion.23, bf16[1,176,1024]{2,1,0:T(8,128)(2,1)S(1)} %copy-done, bf16[1,176,1024]{2,1,0:T(8,128)(2,1)S(1)} %copy-done.8), kind=kOutput, calls=%fused_computation.1 | convolution fusion | flops 4075765760 | bytes 27754496 | tf_op jit(solution)/shard_map/dot_general | solution.py:21
  243.0 0.0 copy-start.4
  243.0 0.0 reduce-scatter.5.cloned.1.call-update
  243.0 96.4 %reduce-scatter.5.cloned.1.call-done = bf16[352,1024]{1,0:T(8,128)(2,1)} async-done(((bf16[5632,1024]{1,0:T(8,128)(2,1)}), bf16[352,1024]{1,0:T(8,128)(2,1)}) %reduce-scatter.5.cloned.1.call-update) | async-done | bytes 720912 | tf_op jit(solution)/shard_map/reduce_scatter | solution.py:74
  339.5 2.1 reshape.115
  341.6 8.3 %all-to-all-start.1 = ((bf16[16,22,1024]{2,1,0:T(8,128)(2,1)}), bf16[16,22,1024]{2,1,0:T(8,128)(2,1)S(1)}, u32[]{:S(2)}, u32[]{:S(2)}) async-start(bf16[16,22,1024]{2,1,0:T(8,128)(2,1)} %reshape.115), calls=%async_computation.2 | async-start | bytes 1572864 | tf_op jit(solution)/shard_map/all_to_all | solution.py:81
  349.9 0.1 copy.32
  350.0 0.1 reshape.118
  350.1 0.1 iota_compare_fusion.2
  350.3 0.1 eq.57
  350.4 0.0 copy-done.4
  350.4 0.3 fusion.37
  350.7 0.0 copy-start.7
  350.7 2.3 gather_fusion
  353.0 0.1 reshape.121
  353.1 0.1 copy.33
  353.2 19.4 %all-to-all-done.1 = bf16[16,22,1024]{2,1,0:T(8,128)(2,1)S(1)} async-done(((bf16[16,22,1024]{2,1,0:T(8,128)(2,1)}), bf16[16,22,1024]{2,1,0:T(8,128)(2,1)S(1)}, u32[]{:S(2)}, u32[]{:S(2)}) %all-to-all-start.1) | async-done | bytes 720928 | tf_op jit(solution)/shard_map/all_to_all | solution.py:81
  372.6 0.2 reshape.129
  372.8 0.4 fusion.12
  373.2 0.2 fusion.13
  373.3 0.0 copy-start.1
  373.4 0.0 copy-done.7
  373.4 0.8 fusion.15
  374.1 0.0 copy-done.1
  (13 shorter events, 0.2 us)
Async XLA Ops:
  7.2 222.7 %copy-start = (bf16[1,176,1024]{2,1,0:T(8,128)(2,1)S(1)}, bf16[1,176,1024]{2,1,0:T(8,128)(2,1)}, u32[]{:S(2)}) copy-start(bf16[1,176,1024]{2,1,0:T(8,128)(2,1)} %param.18) | copy-start | bytes 1081348
  7.2 92.5 %reduce-scatter.7.cloned.1.call-start = ((), (), s32[]{:S(2)}) async-start(), calls=%async_computation.6 | async-start | bytes 6127616
  11.7 0.7 copy-start.5
  11.7 88.1 %copy-start.3 = (bf16[88,1024]{1,0:T(8,128)(2,1)S(1)}, bf16[88,1024]{1,0:T(8,128)(2,1)}, u32[]{:S(2)}) copy-start(bf16[88,1024]{1,0:T(8,128)(2,1)} %param.10) | copy-start | bytes 540676
  11.7 89.2 %copy-start.6 = (f32[1024]{0:T(1024)S(1)}, f32[1024]{0:T(1024)}, u32[]{:S(2)}) copy-start(f32[1024]{0:T(1024)} %param.13) | copy-start | bytes 12292
  11.7 208.0 %all-gather.2.cloned.1.call-start = ((), (), s32[]{:S(2)}) async-start(), calls=%async_computation.4 | async-start | bytes 12255232 | tf_op jit(solution)/shard_map/all_gather | solution.py:72
  100.9 118.8 %copy-start.2 = (bf16[1,176,1024]{2,1,0:T(8,128)(2,1)S(1)}, bf16[1,176,1024]{2,1,0:T(8,128)(2,1)}, u32[]{:S(2)}) copy-start(bf16[1,176,1024]{2,1,0:T(8,128)(2,1)} %param.16) | copy-start | bytes 1081348
  135.1 94.8 %copy-start.8 = (bf16[1,176,1024]{2,1,0:T(8,128)(2,1)S(1)}, bf16[1,176,1024]{2,1,0:T(8,128)(2,1)}, u32[]{:S(2)}) copy-start(bf16[1,176,1024]{2,1,0:T(8,128)(2,1)} %param.17) | copy-start | bytes 1081348
  135.2 204.3 %reduce-scatter.5.cloned.1.call-start = ((), (), s32[]{:S(2)}) async-start(), calls=%async_computation.5 | async-start | bytes 12255232 | tf_op jit(solution)/shard_map/reduce_scatter | solution.py:74
  243.0 107.4 %copy-start.4 = (f32[1024,16]{0,1:T(8,128)S(1)}, f32[1024,16]{0,1:T(8,128)}, u32[]{:S(2)}) copy-start(f32[1024,16]{0,1:T(8,128)} %param.14) | copy-start | bytes 196612
  341.6 31.1 %all-to-all-start.1 = ((bf16[16,22,1024]{2,1,0:T(8,128)(2,1)}), bf16[16,22,1024]{2,1,0:T(8,128)(2,1)S(1)}, u32[]{:S(2)}, u32[]{:S(2)}) async-start(bf16[16,22,1024]{2,1,0:T(8,128)(2,1)} %reshape.115), calls=%async_computation.2 | async-start | bytes 1572864 | tf_op jit(solution)/shard_map/all_to_all | solution.py:81
  350.7 22.7 %copy-start.7 = (f32[1024]{0:T(1024)S(1)}, f32[1024]{0:T(1024)}, u32[]{:S(2)}) copy-start(f32[1024]{0:T(1024)} %param.19) | copy-start | bytes 12292
  373.3 0.8 copy-start.1
Sparse Core Ops, SparseCore 0:
  11.8 87.8 reduce-scatter.6
  135.3 84.3 all-gather.1
  243.2 96.2 reduce-scatter.4
where the time goes:
time: 381 us
  waiting for transfers between devices  287 us (75%)
  blocking collectives  32.1 us (8%)
  matrix products  28.7 us (8%)
  between operations  14 us (4%)
  starting transfers between devices  8.46 us (2%)
  local copies, waits for them, and re-layouts  7.73 us (2%)
    reduce_scatter x1, waiting for transfers between devices, per_device(): lax.psum_scatter(expert_block(block, gate_rows, up_rows, down_rows).astyp...  96.4 us
    unnamed x4, waiting for transfers between devices  86.2 us
    all_gather x1, waiting for transfers between devices, per_device(): all_rows = lax.all_gather(rows_in, 'tensor', axis=0, tiled=True)  84.5 us
    all_to_all x1, blocking collectives, per_device(): lax.all_to_all(send_slots, 'expert', split_axis=0, concat_axis=0, tiled=T...  32.1 us
    all_to_all x1, waiting for transfers between devices, per_device(): lax.all_to_all(expert_out, 'expert', split_axis=0, concat_axis=0, tiled=T...  19.4 us
    dot_general x1, matrix products, expert_block(): return jnp.dot(hid, down_rows, preferred_element_type=jnp.float32)  13.1 us
    dot_general x1, matrix products, expert_block(): lax.dot_general(inputs, gate_rows, (((1,), (1,)), ((), ())), preferred_el...  10.2 us
    all_to_all x1, starting transfers between devices, per_device(): lax.all_to_all(expert_out, 'expert', split_axis=0, concat_axis=0, tiled=T...  8.33 us
  transfers between devices with their start and end apart: 4, of which 4 were waited for; matrix products, arithmetic and copies ran while one was open for 1% of the time, Pallas kernels for 0%

commit v1 on v0

--- a/solution.py
+++ b/solution.py
@@ -69,7 +69,9 @@
     gate_rows = w_gate[0]
     up_rows = w_upward[0]
     down_rows = w_downward[0]
-    all_rows = lax.all_gather(rows_in, "tensor", axis=0, tiled=True)
+    all_rows = jnp.concatenate(
+        lax.all_to_all(jnp.stack([rows_in] * lax.axis_size("tensor")), "tensor", 0, 0), axis=0
+    )
     block = all_rows
     expert_sum = lax.psum_scatter(
         expert_block(block, gate_rows, up_rows, down_rows).astype(jnp.bfloat16),

time: 381 us -> 433 us (1.14)
  blocking collectives: 32.1 us -> 167 us
  waiting for transfers between devices: 287 us -> 198 us
  local copies, waits for them, and re-layouts: 7.73 us -> 16.9 us
    all_to_all x0 -> x1, blocking collectives: none -> 135 us  [per_device(): lax.all_to_all(jnp.stack([rows_in] * lax.axis_size('tensor')), 'tensor',...]
    all_gather x1 -> x0, waiting for transfers between devices: 84.5 us -> none  [per_device(): all_rows = lax.all_gather(rows_in, 'tensor', axis=0, tiled=True)]
    another operation x1 -> x3, local copies, waits for them, and re-layouts: 0.01 us -> 6.04 us  [the longest x2 6.03 us: per_device(): jnp.stack([rows_in] * lax.axis_size('tensor'))]
    unnamed x4 -> x3, waiting for transfers between devices: 86.2 us -> 86.2 us
  transfers between devices with their start and end apart: 4 -> 3, of which waited for: 4 -> 3; matrix products, arithmetic and copies ran while one was open for 1% -> 1% of each run, Pallas kernels for 0% -> 0%
where the time goes in v1:
time: 433 us
  waiting for transfers between devices  198 us (46%)
  blocking collectives  167 us (39%)
  matrix products  24.5 us (6%)
  local copies, waits for them, and re-layouts  16.9 us (4%)
  between operations  14.2 us (3%)
  starting transfers between devices  8.41 us (2%)
    all_to_all x1, blocking collectives, per_device(): lax.all_to_all(jnp.stack([rows_in] * lax.axis_size('tensor')), 'tensor',...  135 us
    reduce_scatter x1, waiting for transfers between devices, per_device(): lax.psum_scatter(expert_block(block, gate_rows, up_rows, down_rows).astyp...  92.6 us
    unnamed x3, waiting for transfers between devices  86.2 us
    all_to_all x1, blocking collectives, per_device(): lax.all_to_all(send_slots, 'expert', split_axis=0, concat_axis=0, tiled=T...  32.1 us
    all_to_all x1, waiting for transfers between devices, per_device(): lax.all_to_all(expert_out, 'expert', split_axis=0, concat_axis=0, tiled=T...  19.4 us
    dot_general x1, matrix products, expert_block(): return jnp.dot(hid, down_rows, preferred_element_type=jnp.float32)  13.2 us
  transfers between devices with their start and end apart: 3, of which 3 were waited for; matrix products, arithmetic and copies ran while one was open for 1% of the time, Pallas kernels for 0%

profile of v1, /device:TPU:1, one launch (start us, length us, event | category | flops | bytes accessed | tf_op | source)
XLA Modules:
  0.0 432.6 jit_solution(5425296063510411442)
XLA Ops:
  7.2 0.0 copy-start
  7.2 0.0 reduce-scatter.7.cloned.1.call-start
  7.2 4.4 %fusion.38 = f32[1408,1024]{1,0:T(8,128)} fusion(bf16[64,1408]{1,0:T(8,128)(2,1)} %param.11, bf16[64,1024]{1,0:T(8,128)(2,1)} %param.12), kind=kOutput, calls=%fused_computation.66 | convolution fusion | flops 184549376 | bytes 6078464 | tf_op jit(solution)/shard_map/dot_general | solution.py:42
  11.7 0.0 copy-start.6
  11.7 0.0 copy-start.4
  11.7 0.0 copy-start.7
  11.7 0.0 reduce-scatter.7.cloned.1.call-update
  11.7 0.0 reduce-scatter.5.cloned.1.call-start
  11.7 0.6 copy-done.6
  12.3 0.1 copy.34
  12.4 0.1 reshape.111
  12.6 0.6 reduce-window.6
  13.2 0.2 slice_reduce_fusion
  13.4 0.1 bitcast_bitcast_fusion
  13.5 86.2 %reduce-scatter.7.cloned.1.call-done = f32[88,1024]{1,0:T(8,128)} async-done(((f32[1408,1024]{1,0:T(8,128)}), f32[88,1024]{1,0:T(8,128)}) %reduce-scatter.7.cloned.1.call-update) | async-done | bytes 360464
  99.7 0.0 copy-done.4
  99.7 1.1 fusion.16
  100.9 0.0 copy-done.7
  100.9 0.1 fusion.18
  101.0 0.2 broadcast_in_dim.7
  101.2 0.1 reshape.114
  101.3 0.3 convolution_convert_fusion.1
  101.7 0.2 reshape.115
  101.9 32.1 %all_to_all.15 = bf16[16,22,1024]{2,1,0:T(8,128)(2,1)S(1)} all-to-all(bf16[16,22,1024]{2,1,0:T(8,128)(2,1)S(1)} %reshape.115), channel_id=1, replica_groups=mesh['expert'=16,'tensor'=16] {'expert'}, dimensions={0} | all-to-all | bytes 1441792 | tf_op jit(solution)/shard_map/all_to_all | solution.py:66
  134.0 0.2 stack_reshape.2
  134.2 5.8 %stack.3 = bf16[16,352,1024]{2,1,0:T(8,128)(2,1)} broadcast(bf16[352,1024]{1,0:T(8,128)(2,1)S(1)} %stack_reshape.2), dimensions={1,2} | broadcast | bytes 12255232 | tf_op jit(solution)/shard_map/stack | solution.py:73
  140.1 0.0 copy-start.3
  140.1 135.1 %all_to_all.16 = bf16[16,352,1024]{2,1,0:T(8,128)(2,1)S(1)} all-to-all(bf16[16,352,1024]{2,1,0:T(8,128)(2,1)} %stack.3), channel_id=1, replica_groups=mesh['expert'=16,'tensor'=16] {'tensor'}, dimensions={0} | all-to-all | bytes 23068672 | tf_op jit(solution)/shard_map/all_to_all | solution.py:73
  275.2 0.0 copy-start.1
  275.2 4.2 copy-done.1
  279.4 0.0 copy-done.3
  279.4 0.0 copy-start.9
  279.4 5.9 %fusion.23 = f32[5632,176]{0,1:T(8,128)} fusion(bf16[5632,1024]{1,0:T(8,128)(2,1)S(1)} %bitcast.36, bf16[1,176,1024]{2,1,0:T(8,128)(2,1)S(1)} %copy-done.3), kind=kOutput, calls=%fused_computation.33 | convolution fusion | flops 2030043136 | bytes 15859712 | tf_op jit(solution)/shard_map/dot_general | solution.py:14
  285.4 0.0 copy-done
  285.4 0.0 copy-done.9
  285.4 13.2 %convolution_convert_fusion = bf16[5632,1024]{1,0:T(8,128)(2,1)} fusion(bf16[5632,1024]{1,0:T(8,128)(2,1)} %bitcast.37, f32[5632,176]{0,1:T(8,128)} %fusion.23, bf16[1,176,1024]{2,1,0:T(8,128)(2,1)S(1)} %copy-done, bf16[1,176,1024]{2,1,0:T(8,128)(2,1)S(1)} %copy-done.9), kind=kOutput, calls=%fused_computation.1 | convolution fusion | flops 4075765760 | bytes 27754496 | tf_op jit(solution)/shard_map/dot_general | solution.py:21
  298.5 0.0 copy-start.5
  298.5 0.0 reduce-scatter.5.cloned.1.call-update
  298.5 92.6 %reduce-scatter.5.cloned.1.call-done = bf16[352,1024]{1,0:T(8,128)(2,1)} async-done(((bf16[5632,1024]{1,0:T(8,128)(2,1)}), bf16[352,1024]{1,0:T(8,128)(2,1)}) %reduce-scatter.5.cloned.1.call-update) | async-done | bytes 720912 | tf_op jit(solution)/shard_map/reduce_scatter | solution.py:76
  391.1 2.1 reshape.117
  393.2 8.3 %all-to-all-start.2 = ((bf16[16,22,1024]{2,1,0:T(8,128)(2,1)}), bf16[16,22,1024]{2,1,0:T(8,128)(2,1)S(1)}, u32[]{:S(2)}, u32[]{:S(2)}) async-start(bf16[16,22,1024]{2,1,0:T(8,128)(2,1)} %reshape.117), calls=%async_computation.3 | async-start | bytes 1572864 | tf_op jit(solution)/shard_map/all_to_all | solution.py:83
  401.5 0.1 copy.32
  401.6 0.1 reshape.120
  401.8 0.1 iota_compare_fusion.2
  401.9 0.1 eq.57
  402.0 0.0 copy-done.5
  402.0 0.3 fusion.37
  402.3 0.0 copy-start.8
  402.3 2.3 gather_fusion
  404.6 0.1 reshape.123
  404.7 0.1 copy.33
  404.8 19.4 %all-to-all-done.2 = bf16[16,22,1024]{2,1,0:T(8,128)(2,1)S(1)} async-done(((bf16[16,22,1024]{2,1,0:T(8,128)(2,1)}), bf16[16,22,1024]{2,1,0:T(8,128)(2,1)S(1)}, u32[]{:S(2)}, u32[]{:S(2)}) %all-to-all-start.2) | async-done | bytes 720928 | tf_op jit(solution)/shard_map/all_to_all | solution.py:83
  424.2 0.2 reshape.131
  424.4 0.4 fusion.12
  424.8 0.2 fusion.13
  425.0 0.0 copy-start.2
  425.0 0.0 copy-done.8
  425.0 0.8 fusion.15
  425.8 0.0 copy-done.2
  (13 shorter events, 0.2 us)
Async XLA Ops:
  7.2 278.2 %copy-start = (bf16[1,176,1024]{2,1,0:T(8,128)(2,1)S(1)}, bf16[1,176,1024]{2,1,0:T(8,128)(2,1)}, u32[]{:S(2)}) copy-start(bf16[1,176,1024]{2,1,0:T(8,128)(2,1)} %param.18) | copy-start | bytes 1081348
  7.2 92.5 %reduce-scatter.7.cloned.1.call-start = ((), (), s32[]{:S(2)}) async-start(), calls=%async_computation.6 | async-start | bytes 6127616
  11.7 0.7 copy-start.6
  11.7 88.1 %copy-start.4 = (bf16[88,1024]{1,0:T(8,128)(2,1)S(1)}, bf16[88,1024]{1,0:T(8,128)(2,1)}, u32[]{:S(2)}) copy-start(bf16[88,1024]{1,0:T(8,128)(2,1)} %param.10) | copy-start | bytes 540676
  11.7 89.2 %copy-start.7 = (f32[1024]{0:T(1024)S(1)}, f32[1024]{0:T(1024)}, u32[]{:S(2)}) copy-start(f32[1024]{0:T(1024)} %param.13) | copy-start | bytes 12292
  11.7 379.4 %reduce-scatter.5.cloned.1.call-start = ((), (), s32[]{:S(2)}) async-start(), calls=%async_computation.5 | async-start | bytes 12255232 | tf_op jit(solution)/shard_map/reduce_scatter | solution.py:76
  140.1 139.4 %copy-start.3 = (bf16[1,176,1024]{2,1,0:T(8,128)(2,1)S(1)}, bf16[1,176,1024]{2,1,0:T(8,128)(2,1)}, u32[]{:S(2)}) copy-start(bf16[1,176,1024]{2,1,0:T(8,128)(2,1)} %param.16) | copy-start | bytes 1081348
  275.2 4.2 copy-start.1
  279.4 5.9 %copy-start.9 = (bf16[1,176,1024]{2,1,0:T(8,128)(2,1)S(1)}, bf16[1,176,1024]{2,1,0:T(8,128)(2,1)}, u32[]{:S(2)}) copy-start(bf16[1,176,1024]{2,1,0:T(8,128)(2,1)} %param.17) | copy-start | bytes 1081348
  298.5 103.5 %copy-start.5 = (f32[1024,16]{0,1:T(8,128)S(1)}, f32[1024,16]{0,1:T(8,128)}, u32[]{:S(2)}) copy-start(f32[1024,16]{0,1:T(8,128)} %param.14) | copy-start | bytes 196612
  393.2 31.1 %all-to-all-start.2 = ((bf16[16,22,1024]{2,1,0:T(8,128)(2,1)}), bf16[16,22,1024]{2,1,0:T(8,128)(2,1)S(1)}, u32[]{:S(2)}, u32[]{:S(2)}) async-start(bf16[16,22,1024]{2,1,0:T(8,128)(2,1)} %reshape.117), calls=%async_computation.3 | async-start | bytes 1572864 | tf_op jit(solution)/shard_map/all_to_all | solution.py:83
  402.3 22.7 %copy-start.8 = (f32[1024]{0:T(1024)S(1)}, f32[1024]{0:T(1024)}, u32[]{:S(2)}) copy-start(f32[1024]{0:T(1024)} %param.19) | copy-start | bytes 12292
  425.0 0.8 copy-start.2
Sparse Core Ops, SparseCore 0:
  11.8 87.8 reduce-scatter.6
  298.7 92.3 reduce-scatter.4
